TPU v7x, 32 devices: a whole 2x2x4 slice. The times are simulated.
32 devices in a mesh: tensor: 4 (over x, core), replica: 4 (over z), fsdp: 2 (over y).
Axes of the slice: x: 2, y: 2, z: 4, core: 2. Of those that a mesh axis runs over, the one named last changes fastest.
Arguments:
- gradients: bfloat16 [4, 128, 28672], P('replica', 'fsdp', 'tensor'), may hold values from -6 to 6
- seeds: int32 [2], replicated, may hold values from 0 to 1073741823
- adam_step: int32 [1], replicated, may hold values from 1 to 8
- first_moment: float32 [128, 28672], P(('fsdp', 'replica'), 'tensor'), may hold values from -0.6 to 0.6
- second_moment: float32 [128, 28672], P(('fsdp', 'replica'), 'tensor'), may hold values from 0.001 to 0.1
Outputs:
- new_first: float32 [128, 28672], P(('fsdp', 'replica'), 'tensor')
- new_second: float32 [128, 28672], P(('fsdp', 'replica'), 'tensor')
- step_update: float32 [128, 28672], P(('fsdp', 'replica'), 'tensor')
All inputs are finite; a program needn't handle non-finite values.
Results may differ from a plain program's by a relative error of at most 0.012.
The roundings to bfloat16 on the way count: a program that leaves them out, or rounds other values in their place, can miss the bound.
Values may be sent and summed in bfloat16 or wider, within the bound.
No kernel may reach another device: no remote copies, remote signals or barrier semaphores. Data moves between devices by JAX's collectives and lax.ppermute only.
A program may use at most 64 MiB of HBM per device.

v0:
```python
import math
import jax
import jax.numpy as jnp
from jax import lax
from jax.sharding import PartitionSpec as P

RANK = 512


def scramble(value):
    value = value ^ lax.shift_right_logical(value, jnp.full_like(value, 16))
    value = value * jnp.int32(-2048144789)
    value = value ^ lax.shift_right_logical(value, jnp.full_like(value, 13))
    value = value * jnp.int32(-1028477387)
    value = value ^ lax.shift_right_logical(value, jnp.full_like(value, 16))
    return value


def projection_block(first_column, columns, rank, seeds):
    seed_key = seeds[0] ^ seeds[1] * jnp.int32(668265263)
    column = lax.broadcasted_iota(jnp.int32, (columns, rank), 0) + first_column
    entry = lax.broadcasted_iota(jnp.int32, (columns, rank), 1)
    counter = (column * jnp.int32(rank) + entry) * jnp.int32(2)
    hash_a = scramble(counter * jnp.int32(-1640531535) ^ seed_key)
    hash_b = scramble((counter + jnp.int32(1)) * jnp.int32(-1640531535) ^ seed_key)
    inverse = 1.0 / 16777216.0
    uniform_a = (
        lax.shift_right_logical(hash_a, jnp.full_like(hash_a, 8)).astype(jnp.float32) + 0.5
    ) * inverse
    uniform_b = (
        lax.shift_right_logical(hash_b, jnp.full_like(hash_b, 8)).astype(jnp.float32) + 0.5
    ) * inverse
    gauss = jnp.sqrt(-2.0 * jnp.log(uniform_a)) * jnp.cos(6.283185307179586 * uniform_b)
    return (gauss * rank ** (-0.5)).astype(jnp.bfloat16)


def per_device(gradients, seeds, adam_step, first_moment, second_moment):
    gradient = gradients[0]
    columns = gradient.shape[1]
    replicas = lax.axis_size("replica")
    column_start = lax.axis_index("tensor") * jnp.int32(columns)
    piece_cols = math.gcd(columns, 512)
    blocks = columns // piece_cols
    starts = column_start + lax.iota(jnp.int32, blocks) * jnp.int32(piece_cols)
    tiles = lax.map(lambda first: projection_block(first, piece_cols, RANK, seeds), starts)
    projection = tiles.reshape(columns, RANK)
    partial_value = jnp.dot(gradient, projection, preferred_element_type=jnp.float32) * (
        1.0 / replicas
    )
    share = lax.psum_scatter(partial_value, "replica", scatter_dimension=0, tiled=True)
    sketch = lax.psum(share, "tensor")
    sketch_rounded = sketch.astype(jnp.bfloat16)
    estimate = lax.dot_general(
        sketch_rounded, projection, (((1,), (1,)), ((), ())), preferred_element_type=jnp.float32
    )
    new_first = 0.9 * first_moment + 0.1 * estimate
    new_second = 0.95 * second_moment + 0.05 * estimate * estimate
    step_float = adam_step[0].astype(jnp.float32)
    fix_first = 1.0 - jnp.power(jnp.float32(0.9), step_float)
    fix_second = 1.0 - jnp.power(jnp.float32(0.95), step_float)
    step_update = new_first / fix_first / (jnp.sqrt(new_second / fix_second) + 1e-08)
    return (new_first, new_second, step_update)


def solution(mesh):
    placed = (
        P("replica", "fsdp", "tensor"),
        P(),
        P(),
        P(("fsdp", "replica"), "tensor"),
        P(("fsdp", "replica"), "tensor"),
    )
    return jax.shard_map(
        per_device,
        mesh=mesh,
        in_specs=placed,
        out_specs=(
            P(("fsdp", "replica"), "tensor"),
            P(("fsdp", "replica"), "tensor"),
            P(("fsdp", "replica"), "tensor"),
        ),
        check_vma=False,
    )
```

profile of v0, /device:TPU:1, one launch (start us, length us, event | category | flops | bytes accessed | tf_op | source)
XLA Modules:
  0.0 164.6 jit_solution(9987295474891056560)
XLA Ops:
  7.2 1.3 fusion.26
  9.9 99.4 %while.12 = (s32[]{:T(128)}, bf16[14,512,512]{2,1,0:T(8,128)(2,1)}, s32[14]{0:T(128)S(1)}, s32[]{:T(128)}, s32[]{:T(128)}) while((s32[]{:T(128)}, bf16[14,512,512]{2,1,0:T(8,128)(2,1)}, s32[14]{0:T(128)S(1)}, s32[]{:T(128)}, s32[]{:T(128)}) %tuple.33), condition=%wide.region_1.2_spmd, body=%wide.region_0.1_spmd.sunk | while | flops 9176066 | bytes 529485 | solution.py:45
  11.1 5.9 %fusion.31 = bf16[14,512,512]{2,1,0:T(8,128)(2,1)} fusion(bf16[14,512,512]{2,1,0:T(8,128)(2,1)} %get-tuple-element.105, s32[]{:T(128)} %get-tuple-element.104, s32[]{:T(128)} %get-tuple-element.112, s32[512]{0:T(512)S(1)} %add_multiply_fusion.2), kind=kLoop, calls=%fused_computation.25.clone.1 | loop fusion | flops 9175040 | bytes 527360 | tf_op jit(solution)/shard_map/while/body/jit(dynamic_update_index_in_dim)/dynamic_update_slice | solution.py:45
  17.6 0.6 add_multiply_fusion.2
  18.2 5.9 %fusion.31 = bf16[14,512,512]{2,1,0:T(8,128)(2,1)} fusion(bf16[14,512,512]{2,1,0:T(8,128)(2,1)} %get-tuple-element.105, s32[]{:T(128)} %get-tuple-element.104, s32[]{:T(128)} %get-tuple-element.112, s32[512]{0:T(512)S(1)} %add_multiply_fusion.2), kind=kLoop, calls=%fused_computation.25.clone.1 | loop fusion | flops 9175040 | bytes 527360 | tf_op jit(solution)/shard_map/while/body/jit(dynamic_update_index_in_dim)/dynamic_update_slice | solution.py:45
  25.3 5.9 %fusion.31 = bf16[14,512,512]{2,1,0:T(8,128)(2,1)} fusion(bf16[14,512,512]{2,1,0:T(8,128)(2,1)} %get-tuple-element.105, s32[]{:T(128)} %get-tuple-element.104, s32[]{:T(128)} %get-tuple-element.112, s32[512]{0:T(512)S(1)} %add_multiply_fusion.2), kind=kLoop, calls=%fused_computation.25.clone.1 | loop fusion | flops 9175040 | bytes 527360 | tf_op jit(solution)/shard_map/while/body/jit(dynamic_update_index_in_dim)/dynamic_update_slice | solution.py:45
  31.8 0.6 add_multiply_fusion.2
  32.4 5.9 %fusion.31 = bf16[14,512,512]{2,1,0:T(8,128)(2,1)} fusion(bf16[14,512,512]{2,1,0:T(8,128)(2,1)} %get-tuple-element.105, s32[]{:T(128)} %get-tuple-element.104, s32[]{:T(128)} %get-tuple-element.112, s32[512]{0:T(512)S(1)} %add_multiply_fusion.2), kind=kLoop, calls=%fused_computation.25.clone.1 | loop fusion | flops 9175040 | bytes 527360 | tf_op jit(solution)/shard_map/while/body/jit(dynamic_update_index_in_dim)/dynamic_update_slice | solution.py:45
  38.9 0.6 add_multiply_fusion.2
  39.5 5.8 %fusion.31 = bf16[14,512,512]{2,1,0:T(8,128)(2,1)} fusion(bf16[14,512,512]{2,1,0:T(8,128)(2,1)} %get-tuple-element.105, s32[]{:T(128)} %get-tuple-element.104, s32[]{:T(128)} %get-tuple-element.112, s32[512]{0:T(512)S(1)} %add_multiply_fusion.2), kind=kLoop, calls=%fused_computation.25.clone.1 | loop fusion | flops 9175040 | bytes 527360 | tf_op jit(solution)/shard_map/while/body/jit(dynamic_update_index_in_dim)/dynamic_update_slice | solution.py:45
  46.0 0.6 add_multiply_fusion.2
  46.6 5.9 %fusion.31 = bf16[14,512,512]{2,1,0:T(8,128)(2,1)} fusion(bf16[14,512,512]{2,1,0:T(8,128)(2,1)} %get-tuple-element.105, s32[]{:T(128)} %get-tuple-element.104, s32[]{:T(128)} %get-tuple-element.112, s32[512]{0:T(512)S(1)} %add_multiply_fusion.2), kind=kLoop, calls=%fused_computation.25.clone.1 | loop fusion | flops 9175040 | bytes 527360 | tf_op jit(solution)/shard_map/while/body/jit(dynamic_update_index_in_dim)/dynamic_update_slice | solution.py:45
  53.0 0.6 add_multiply_fusion.2
  53.7 5.9 %fusion.31 = bf16[14,512,512]{2,1,0:T(8,128)(2,1)} fusion(bf16[14,512,512]{2,1,0:T(8,128)(2,1)} %get-tuple-element.105, s32[]{:T(128)} %get-tuple-element.104, s32[]{:T(128)} %get-tuple-element.112, s32[512]{0:T(512)S(1)} %add_multiply_fusion.2), kind=kLoop, calls=%fused_computation.25.clone.1 | loop fusion | flops 9175040 | bytes 527360 | tf_op jit(solution)/shard_map/while/body/jit(dynamic_update_index_in_dim)/dynamic_update_slice | solution.py:45
  60.1 0.6 add_multiply_fusion.2
  60.8 5.9 %fusion.31 = bf16[14,512,512]{2,1,0:T(8,128)(2,1)} fusion(bf16[14,512,512]{2,1,0:T(8,128)(2,1)} %get-tuple-element.105, s32[]{:T(128)} %get-tuple-element.104, s32[]{:T(128)} %get-tuple-element.112, s32[512]{0:T(512)S(1)} %add_multiply_fusion.2), kind=kLoop, calls=%fused_computation.25.clone.1 | loop fusion | flops 9175040 | bytes 527360 | tf_op jit(solution)/shard_map/while/body/jit(dynamic_update_index_in_dim)/dynamic_update_slice | solution.py:45
  67.2 0.6 add_multiply_fusion.2
  67.9 5.9 %fusion.31 = bf16[14,512,512]{2,1,0:T(8,128)(2,1)} fusion(bf16[14,512,512]{2,1,0:T(8,128)(2,1)} %get-tuple-element.105, s32[]{:T(128)} %get-tuple-element.104, s32[]{:T(128)} %get-tuple-element.112, s32[512]{0:T(512)S(1)} %add_multiply_fusion.2), kind=kLoop, calls=%fused_computation.25.clone.1 | loop fusion | flops 9175040 | bytes 527360 | tf_op jit(solution)/shard_map/while/body/jit(dynamic_update_index_in_dim)/dynamic_update_slice | solution.py:45
  74.3 0.6 add_multiply_fusion.2
  75.0 5.9 %fusion.31 = bf16[14,512,512]{2,1,0:T(8,128)(2,1)} fusion(bf16[14,512,512]{2,1,0:T(8,128)(2,1)} %get-tuple-element.105, s32[]{:T(128)} %get-tuple-element.104, s32[]{:T(128)} %get-tuple-element.112, s32[512]{0:T(512)S(1)} %add_multiply_fusion.2), kind=kLoop, calls=%fused_computation.25.clone.1 | loop fusion | flops 9175040 | bytes 527360 | tf_op jit(solution)/shard_map/while/body/jit(dynamic_update_index_in_dim)/dynamic_update_slice | solution.py:45
  82.1 5.9 %fusion.31 = bf16[14,512,512]{2,1,0:T(8,128)(2,1)} fusion(bf16[14,512,512]{2,1,0:T(8,128)(2,1)} %get-tuple-element.105, s32[]{:T(128)} %get-tuple-element.104, s32[]{:T(128)} %get-tuple-element.112, s32[512]{0:T(512)S(1)} %add_multiply_fusion.2), kind=kLoop, calls=%fused_computation.25.clone.1 | loop fusion | flops 9175040 | bytes 527360 | tf_op jit(solution)/shard_map/while/body/jit(dynamic_update_index_in_dim)/dynamic_update_slice | solution.py:45
  88.5 0.6 add_multiply_fusion.2
  89.2 5.9 %fusion.31 = bf16[14,512,512]{2,1,0:T(8,128)(2,1)} fusion(bf16[14,512,512]{2,1,0:T(8,128)(2,1)} %get-tuple-element.105, s32[]{:T(128)} %get-tuple-element.104, s32[]{:T(128)} %get-tuple-element.112, s32[512]{0:T(512)S(1)} %add_multiply_fusion.2), kind=kLoop, calls=%fused_computation.25.clone.1 | loop fusion | flops 9175040 | bytes 527360 | tf_op jit(solution)/shard_map/while/body/jit(dynamic_update_index_in_dim)/dynamic_update_slice | solution.py:45
  95.6 0.6 add_multiply_fusion.2
  96.3 5.9 %fusion.31 = bf16[14,512,512]{2,1,0:T(8,128)(2,1)} fusion(bf16[14,512,512]{2,1,0:T(8,128)(2,1)} %get-tuple-element.105, s32[]{:T(128)} %get-tuple-element.104, s32[]{:T(128)} %get-tuple-element.112, s32[512]{0:T(512)S(1)} %add_multiply_fusion.2), kind=kLoop, calls=%fused_computation.25.clone.1 | loop fusion | flops 9175040 | bytes 527360 | tf_op jit(solution)/shard_map/while/body/jit(dynamic_update_index_in_dim)/dynamic_update_slice | solution.py:45
  103.4 5.9 %fusion.31 = bf16[14,512,512]{2,1,0:T(8,128)(2,1)} fusion(bf16[14,512,512]{2,1,0:T(8,128)(2,1)} %get-tuple-element.105, s32[]{:T(128)} %get-tuple-element.104, s32[]{:T(128)} %get-tuple-element.112, s32[512]{0:T(512)S(1)} %add_multiply_fusion.2), kind=kLoop, calls=%fused_computation.25.clone.1 | loop fusion | flops 9175040 | bytes 527360 | tf_op jit(solution)/shard_map/while/body/jit(dynamic_update_index_in_dim)/dynamic_update_slice | solution.py:45
  109.2 5.2 %fusion.20 = f32[64,512]{0,1:T(8,128)S(1)} fusion(bf16[7168,512]{1,0:T(8,128)(2,1)} %bitcast.16, bf16[1,64,7168]{2,1,0:T(8,128)(2,1)S(1)} %copy-done), kind=kOutput, calls=%fused_computation.28 | convolution fusion | flops 469794816 | bytes 8388608 | tf_op jit(solution)/shard_map/dot_general | solution.py:47
  114.4 0.8 copy.8
  116.0 18.6 %reduce-scatter.4.cloned.1.call-done = f32[16,512]{1,0:T(8,128)} async-done(((f32[64,512]{1,0:T(8,128)}), f32[16,512]{1,0:T(8,128)}) %reduce-scatter.4.cloned.1.call-update) | async-done | bytes 32784
  134.5 0.9 copy.9
  135.4 16.2 %psum.7 = bf16[16,512]{0,1:T(8,128)(2,1)S(1)} all-reduce(f32[16,512]{0,1:T(8,128)S(1)} %copy.9), channel_id=1, replica_groups=mesh['tensor'=4,'replica'=4,'fsdp'=2] {'tensor'}, use_global_device_ids=true, to_apply=%region_3.4 | all-reduce | flops 8192 | bytes 49152 | tf_op jit(solution)/shard_map/psum | solution.py:51
  151.6 6.2 %multiply_divide_fusion = (f32[16,7168]{1,0:T(8,128)}, f32[16,7168]{1,0:T(8,128)}, f32[16,7168]{1,0:T(8,128)}) fusion(f32[]{:T(128)} %bitcast.6, f32[]{:T(128)} %bitcast.5, f32[16,7168]{1,0:T(8,128)S(1)} %copy-done.1, f32[16,7168]{1,0:T(8,128)S(1)} %copy-done.2, bf16[16,512]{0,1:T(8,128)(2,1)S(1)} %psum.7, bf16[7168,512]{1,0:T(8,128)(2,1)} %bitcast.17), kind=kOutput, calls=%fused_computation.32 | convolution fusion | flops 118702080 | bytes 9650184 | tf_op jit(solution)/shard_map/dot_general | solution.py:53
  (28 shorter events, 10.8 us)
Async XLA Ops:
  7.2 102.1 %copy-start = (bf16[1,64,7168]{2,1,0:T(8,128)(2,1)S(1)}, bf16[1,64,7168]{2,1,0:T(8,128)(2,1)}, u32[]{:S(2)}) copy-start(bf16[1,64,7168]{2,1,0:T(8,128)(2,1)} %param.7) | copy-start | bytes 2752516
  7.2 127.3 %reduce-scatter.4.cloned.1.call-start = ((), (), s32[]{:S(2)}) async-start(), calls=%async_computation.1 | async-start | bytes 163840
  9.9 141.7 %copy-start.1 = (f32[16,7168]{1,0:T(8,128)S(1)}, f32[16,7168]{1,0:T(8,128)}, u32[]{:S(2)}) copy-start(f32[16,7168]{1,0:T(8,128)} %param.11) | copy-start | bytes 1376260
  9.9 141.7 %copy-start.2 = (f32[16,7168]{1,0:T(8,128)S(1)}, f32[16,7168]{1,0:T(8,128)}, u32[]{:S(2)}) copy-start(f32[16,7168]{1,0:T(8,128)} %param.10) | copy-start | bytes 1376260
Sparse Core Ops, SparseCore 0:
  115.3 19.1 reduce-scatter.3
where the time goes:
time: 165 us
  other arithmetic  91.1 us (55%)
  waiting for transfers between devices  18.6 us (11%)
  blocking collectives  16.2 us (10%)
  between operations  16.1 us (10%)
  matrix products  11.4 us (7%)
  local copies, waits for them, and re-layouts  11.2 us (7%)
    dynamic_update_slice x14, other arithmetic, per_device(): lax.map(lambda first: projection_block(first, piece_cols, RANK, seeds), s...  82 us
    unnamed x2, waiting for transfers between devices  18.6 us
    psum x1, blocking collectives, per_device(): sketch = lax.psum(share, 'tensor')  16.2 us
    mul x14, other arithmetic, projection_block(): counter = (column * jnp.int32(rank) + entry) * jnp.int32(2)  9.07 us
    dynamic_slice x14, local copies, waits for them, and re-layouts, per_device(): lax.map(lambda first: projection_block(first, piece_cols, RANK, seeds), s...  8.15 us
    dot_general x1, matrix products, per_device(): lax.dot_general(sketch_rounded, projection, (((1,), (1,)), ((), ())), pre...  6.19 us
    dot_general x1, matrix products, per_device(): jnp.dot(gradient, projection, preferred_element_type=jnp.float32)  5.17 us
  transfers between devices with their start and end apart: 1, of which 1 were waited for; matrix products, arithmetic and copies ran while one was open for 0% of the time, Pallas kernels for 0%

commit v1 on v0

--- a/solution.py
+++ b/solution.py
@@ -48,7 +48,7 @@
         1.0 / replicas
     )
     share = lax.psum_scatter(partial_value, "replica", scatter_dimension=0, tiled=True)
-    sketch = lax.psum(share, "tensor")
+    sketch = lax.all_gather(share, "tensor").sum(axis=0)
     sketch_rounded = sketch.astype(jnp.bfloat16)
     estimate = lax.dot_general(
         sketch_rounded, projection, (((1,), (1,)), ((), ())), preferred_element_type=jnp.float32

time: 165 us -> 156 us (0.945)
  blocking collectives: 16.2 us -> 8.49 us
  local copies, waits for them, and re-layouts: 11.2 us -> 9.49 us
    reduce_scatter x0 -> x1, waiting for transfers between devices: none -> 18.6 us  [per_device(): lax.psum_scatter(partial_value, 'replica', scatter_dimension=0, tiled=True)]
    unnamed x2 -> x1, waiting for transfers between devices: 18.6 us -> 0.02 us
    psum x1 -> x0, blocking collectives: 16.2 us -> none  [per_device(): sketch = lax.psum(share, 'tensor')]
    all_gather x0 -> x1, blocking collectives: none -> 8.49 us  [per_device(): sketch = lax.all_gather(share, 'tensor').sum(axis=0)]
    unnamed x8 -> x6, local copies, waits for them, and re-layouts: 1.67 us -> 0.02 us
where the time goes in v1:
time: 156 us; the launch traced here: 155 us
  other arithmetic  91.1 us (58%)
  waiting for transfers between devices  18.6 us (12%)
  between operations  16.1 us (10%)
  matrix products  11.4 us (7%)
  local copies, waits for them, and re-layouts  9.49 us (6%)
  blocking collectives  8.49 us (5%)
    dynamic_update_slice x14, other arithmetic, per_device(): lax.map(lambda first: projection_block(first, piece_cols, RANK, seeds), s...  82 us
    reduce_scatter x1, waiting for transfers between devices, per_device(): lax.psum_scatter(partial_value, 'replica', scatter_dimension=0, tiled=True)  18.6 us
    mul x14, other arithmetic, projection_block(): counter = (column * jnp.int32(rank) + entry) * jnp.int32(2)  9.07 us
    all_gather x1, blocking collectives, per_device(): sketch = lax.all_gather(share, 'tensor').sum(axis=0)  8.49 us
    dynamic_slice x14, local copies, waits for them, and re-layouts, per_device(): lax.map(lambda first: projection_block(first, piece_cols, RANK, seeds), s...  8.15 us
    dot_general x1, matrix products, per_device(): lax.dot_general(sketch_rounded, projection, (((1,), (1,)), ((), ())), pre...  6.19 us
    dot_general x1, matrix products, per_device(): jnp.dot(gradient, projection, preferred_element_type=jnp.float32)  5.2 us
  transfers between devices with their start and end apart: 1, of which 1 were waited for; matrix products, arithmetic and copies ran while one was open for 0% of the time, Pallas kernels for 0%

profile of v1, /device:TPU:1, one launch (start us, length us, event | category | flops | bytes accessed | tf_op | source)
XLA Modules:
  0.0 155.3 jit_solution(15997003003464879319)
XLA Ops:
  7.2 1.3 fusion.26
  9.9 99.4 %while.12 = (s32[]{:T(128)}, bf16[14,512,512]{2,1,0:T(8,128)(2,1)}, s32[14]{0:T(128)S(1)}, s32[]{:T(128)}, s32[]{:T(128)}) while((s32[]{:T(128)}, bf16[14,512,512]{2,1,0:T(8,128)(2,1)}, s32[14]{0:T(128)S(1)}, s32[]{:T(128)}, s32[]{:T(128)}) %tuple.33), condition=%wide.region_1.2_spmd, body=%wide.region_0.1_spmd.sunk | while | flops 9176066 | bytes 529485 | solution.py:45
  10.5 0.6 add_multiply_fusion.2
  11.1 5.9 %fusion.31 = bf16[14,512,512]{2,1,0:T(8,128)(2,1)} fusion(bf16[14,512,512]{2,1,0:T(8,128)(2,1)} %get-tuple-element.105, s32[]{:T(128)} %get-tuple-element.104, s32[]{:T(128)} %get-tuple-element.112, s32[512]{0:T(512)S(1)} %add_multiply_fusion.2), kind=kLoop, calls=%fused_computation.25.clone.1 | loop fusion | flops 9175040 | bytes 527360 | tf_op jit(solution)/shard_map/while/body/jit(dynamic_update_index_in_dim)/dynamic_update_slice | solution.py:45
  17.6 0.6 add_multiply_fusion.2
  18.2 5.9 %fusion.31 = bf16[14,512,512]{2,1,0:T(8,128)(2,1)} fusion(bf16[14,512,512]{2,1,0:T(8,128)(2,1)} %get-tuple-element.105, s32[]{:T(128)} %get-tuple-element.104, s32[]{:T(128)} %get-tuple-element.112, s32[512]{0:T(512)S(1)} %add_multiply_fusion.2), kind=kLoop, calls=%fused_computation.25.clone.1 | loop fusion | flops 9175040 | bytes 527360 | tf_op jit(solution)/shard_map/while/body/jit(dynamic_update_index_in_dim)/dynamic_update_slice | solution.py:45
  24.7 0.6 add_multiply_fusion.2
  25.3 5.9 %fusion.31 = bf16[14,512,512]{2,1,0:T(8,128)(2,1)} fusion(bf16[14,512,512]{2,1,0:T(8,128)(2,1)} %get-tuple-element.105, s32[]{:T(128)} %get-tuple-element.104, s32[]{:T(128)} %get-tuple-element.112, s32[512]{0:T(512)S(1)} %add_multiply_fusion.2), kind=kLoop, calls=%fused_computation.25.clone.1 | loop fusion | flops 9175040 | bytes 527360 | tf_op jit(solution)/shard_map/while/body/jit(dynamic_update_index_in_dim)/dynamic_update_slice | solution.py:45
  31.7 0.6 add_multiply_fusion.2
  32.4 5.9 %fusion.31 = bf16[14,512,512]{2,1,0:T(8,128)(2,1)} fusion(bf16[14,512,512]{2,1,0:T(8,128)(2,1)} %get-tuple-element.105, s32[]{:T(128)} %get-tuple-element.104, s32[]{:T(128)} %get-tuple-element.112, s32[512]{0:T(512)S(1)} %add_multiply_fusion.2), kind=kLoop, calls=%fused_computation.25.clone.1 | loop fusion | flops 9175040 | bytes 527360 | tf_op jit(solution)/shard_map/while/body/jit(dynamic_update_index_in_dim)/dynamic_update_slice | solution.py:45
  38.8 0.6 add_multiply_fusion.2
  39.5 5.8 %fusion.31 = bf16[14,512,512]{2,1,0:T(8,128)(2,1)} fusion(bf16[14,512,512]{2,1,0:T(8,128)(2,1)} %get-tuple-element.105, s32[]{:T(128)} %get-tuple-element.104, s32[]{:T(128)} %get-tuple-element.112, s32[512]{0:T(512)S(1)} %add_multiply_fusion.2), kind=kLoop, calls=%fused_computation.25.clone.1 | loop fusion | flops 9175040 | bytes 527360 | tf_op jit(solution)/shard_map/while/body/jit(dynamic_update_index_in_dim)/dynamic_update_slice | solution.py:45
  45.9 0.6 add_multiply_fusion.2
  46.6 5.9 %fusion.31 = bf16[14,512,512]{2,1,0:T(8,128)(2,1)} fusion(bf16[14,512,512]{2,1,0:T(8,128)(2,1)} %get-tuple-element.105, s32[]{:T(128)} %get-tuple-element.104, s32[]{:T(128)} %get-tuple-element.112, s32[512]{0:T(512)S(1)} %add_multiply_fusion.2), kind=kLoop, calls=%fused_computation.25.clone.1 | loop fusion | flops 9175040 | bytes 527360 | tf_op jit(solution)/shard_map/while/body/jit(dynamic_update_index_in_dim)/dynamic_update_slice | solution.py:45
  53.0 0.6 add_multiply_fusion.2
  53.7 5.9 %fusion.31 = bf16[14,512,512]{2,1,0:T(8,128)(2,1)} fusion(bf16[14,512,512]{2,1,0:T(8,128)(2,1)} %get-tuple-element.105, s32[]{:T(128)} %get-tuple-element.104, s32[]{:T(128)} %get-tuple-element.112, s32[512]{0:T(512)S(1)} %add_multiply_fusion.2), kind=kLoop, calls=%fused_computation.25.clone.1 | loop fusion | flops 9175040 | bytes 527360 | tf_op jit(solution)/shard_map/while/body/jit(dynamic_update_index_in_dim)/dynamic_update_slice | solution.py:45
  60.1 0.6 add_multiply_fusion.2
  60.8 5.9 %fusion.31 = bf16[14,512,512]{2,1,0:T(8,128)(2,1)} fusion(bf16[14,512,512]{2,1,0:T(8,128)(2,1)} %get-tuple-element.105, s32[]{:T(128)} %get-tuple-element.104, s32[]{:T(128)} %get-tuple-element.112, s32[512]{0:T(512)S(1)} %add_multiply_fusion.2), kind=kLoop, calls=%fused_computation.25.clone.1 | loop fusion | flops 9175040 | bytes 527360 | tf_op jit(solution)/shard_map/while/body/jit(dynamic_update_index_in_dim)/dynamic_update_slice | solution.py:45
  67.2 0.6 add_multiply_fusion.2
  67.9 5.9 %fusion.31 = bf16[14,512,512]{2,1,0:T(8,128)(2,1)} fusion(bf16[14,512,512]{2,1,0:T(8,128)(2,1)} %get-tuple-element.105, s32[]{:T(128)} %get-tuple-element.104, s32[]{:T(128)} %get-tuple-element.112, s32[512]{0:T(512)S(1)} %add_multiply_fusion.2), kind=kLoop, calls=%fused_computation.25.clone.1 | loop fusion | flops 9175040 | bytes 527360 | tf_op jit(solution)/shard_map/while/body/jit(dynamic_update_index_in_dim)/dynamic_update_slice | solution.py:45
  74.3 0.6 add_multiply_fusion.2
  75.0 5.9 %fusion.31 = bf16[14,512,512]{2,1,0:T(8,128)(2,1)} fusion(bf16[14,512,512]{2,1,0:T(8,128)(2,1)} %get-tuple-element.105, s32[]{:T(128)} %get-tuple-element.104, s32[]{:T(128)} %get-tuple-element.112, s32[512]{0:T(512)S(1)} %add_multiply_fusion.2), kind=kLoop, calls=%fused_computation.25.clone.1 | loop fusion | flops 9175040 | bytes 527360 | tf_op jit(solution)/shard_map/while/body/jit(dynamic_update_index_in_dim)/dynamic_update_slice | solution.py:45
  81.4 0.6 add_multiply_fusion.2
  82.1 5.9 %fusion.31 = bf16[14,512,512]{2,1,0:T(8,128)(2,1)} fusion(bf16[14,512,512]{2,1,0:T(8,128)(2,1)} %get-tuple-element.105, s32[]{:T(128)} %get-tuple-element.104, s32[]{:T(128)} %get-tuple-element.112, s32[512]{0:T(512)S(1)} %add_multiply_fusion.2), kind=kLoop, calls=%fused_computation.25.clone.1 | loop fusion | flops 9175040 | bytes 527360 | tf_op jit(solution)/shard_map/while/body/jit(dynamic_update_index_in_dim)/dynamic_update_slice | solution.py:45
  89.2 5.9 %fusion.31 = bf16[14,512,512]{2,1,0:T(8,128)(2,1)} fusion(bf16[14,512,512]{2,1,0:T(8,128)(2,1)} %get-tuple-element.105, s32[]{:T(128)} %get-tuple-element.104, s32[]{:T(128)} %get-tuple-element.112, s32[512]{0:T(512)S(1)} %add_multiply_fusion.2), kind=kLoop, calls=%fused_computation.25.clone.1 | loop fusion | flops 9175040 | bytes 527360 | tf_op jit(solution)/shard_map/while/body/jit(dynamic_update_index_in_dim)/dynamic_update_slice | solution.py:45
  96.3 5.9 %fusion.31 = bf16[14,512,512]{2,1,0:T(8,128)(2,1)} fusion(bf16[14,512,512]{2,1,0:T(8,128)(2,1)} %get-tuple-element.105, s32[]{:T(128)} %get-tuple-element.104, s32[]{:T(128)} %get-tuple-element.112, s32[512]{0:T(512)S(1)} %add_multiply_fusion.2), kind=kLoop, calls=%fused_computation.25.clone.1 | loop fusion | flops 9175040 | bytes 527360 | tf_op jit(solution)/shard_map/while/body/jit(dynamic_update_index_in_dim)/dynamic_update_slice | solution.py:45
  102.7 0.6 add_multiply_fusion.2
  103.4 5.9 %fusion.31 = bf16[14,512,512]{2,1,0:T(8,128)(2,1)} fusion(bf16[14,512,512]{2,1,0:T(8,128)(2,1)} %get-tuple-element.105, s32[]{:T(128)} %get-tuple-element.104, s32[]{:T(128)} %get-tuple-element.112, s32[512]{0:T(512)S(1)} %add_multiply_fusion.2), kind=kLoop, calls=%fused_computation.25.clone.1 | loop fusion | flops 9175040 | bytes 527360 | tf_op jit(solution)/shard_map/while/body/jit(dynamic_update_index_in_dim)/dynamic_update_slice | solution.py:45
  109.2 5.2 %fusion.20 = f32[64,512]{1,0:T(8,128)} fusion(bf16[7168,512]{1,0:T(8,128)(2,1)} %bitcast.16, bf16[1,64,7168]{2,1,0:T(8,128)(2,1)S(1)} %copy-done), kind=kOutput, calls=%fused_computation.28 | convolution fusion | flops 469794816 | bytes 8388608 | tf_op jit(solution)/shard_map/dot_general | solution.py:47
  115.2 18.6 %reduce-scatter.2.cloned.1.call-done = f32[16,512]{1,0:T(8,128)} async-done(((f32[64,512]{1,0:T(8,128)}), f32[16,512]{1,0:T(8,128)}) %reduce-scatter.2.cloned.1.call-update) | async-done | bytes 32784 | tf_op jit(solution)/shard_map/reduce_scatter | solution.py:50
  133.7 8.5 %all-gather = f32[64,512]{1,0:T(8,128)S(1)} all-gather(f32[16,512]{1,0:T(8,128)} %reduce-scatter.2.cloned.1.call-done), channel_id=2, replica_groups=mesh['tensor'=4,'replica'=4,'fsdp'=2] {'tensor'}, dimensions={0}, use_global_device_ids=true | all-gather | bytes 163840 | tf_op jit(solution)/shard_map/all_gather | solution.py:51
  142.3 6.2 %multiply_divide_fusion = (f32[16,7168]{1,0:T(8,128)}, f32[16,7168]{1,0:T(8,128)}, f32[16,7168]{1,0:T(8,128)}) fusion(f32[]{:T(128)} %bitcast.7, f32[]{:T(128)} %bitcast.6, f32[16,7168]{1,0:T(8,128)S(1)} %copy-done.1, f32[16,7168]{1,0:T(8,128)S(1)} %copy-done.2, bf16[16,512]{1,0:T(8,128)(2,1)S(1)} %reduce_sum.9, bf16[7168,512]{1,0:T(8,128)(2,1)} %bitcast.17), kind=kOutput, calls=%fused_computation.32 | convolution fusion | flops 118702080 | bytes 9650184 | tf_op jit(solution)/shard_map/dot_general | solution.py:53
  (27 shorter events, 9.5 us)
Async XLA Ops:
  7.2 102.1 %copy-start = (bf16[1,64,7168]{2,1,0:T(8,128)(2,1)S(1)}, bf16[1,64,7168]{2,1,0:T(8,128)(2,1)}, u32[]{:S(2)}) copy-start(bf16[1,64,7168]{2,1,0:T(8,128)(2,1)} %param.7) | copy-start | bytes 2752516
  7.2 126.6 %reduce-scatter.2.cloned.1.call-start = ((), (), s32[]{:S(2)}) async-start(), calls=%async_computation.1 | async-start | bytes 163840 | tf_op jit(solution)/shard_map/reduce_scatter | solution.py:50
  109.2 33.0 %copy-start.1 = (f32[16,7168]{1,0:T(8,128)S(1)}, f32[16,7168]{1,0:T(8,128)}, u32[]{:S(2)}) copy-start(f32[16,7168]{1,0:T(8,128)} %param.11) | copy-start | bytes 1376260
  109.2 33.0 %copy-start.2 = (f32[16,7168]{1,0:T(8,128)S(1)}, f32[16,7168]{1,0:T(8,128)}, u32[]{:S(2)}) copy-start(f32[16,7168]{1,0:T(8,128)} %param.10) | copy-start | bytes 1376260
Sparse Core Ops, SparseCore 0:
  114.6 19.1 reduce-scatter.1
